TPU v7x, 256 devices: a whole 4x4x8 slice. The times are simulated.
256 devices in a mesh: layer: 32 (over z, x), row: 2 (over core), col: 4 (over y).
Axes of the slice: x: 4, y: 4, z: 8, core: 2. Of those that a mesh axis runs over, the one named last changes fastest.
Arguments:
- left_factor: float32 [2048, 65536], P('row', ('layer', 'col')), may hold values from -6 to 6
- right_factor: float32 [65536, 4096], P(('layer', 'row'), 'col'), may hold values from -0.15625 to 0.15625
- left_pattern: int32 [32, 1024], P('row', ('layer', 'col')), may hold values 0 or 1
- right_pattern: int32 [1024, 64], P(('layer', 'row'), 'col'), may hold values 0 or 1
- product_pattern: int32 [32, 64], P('row', 'col'), may hold values 0 or 1
Outputs:
- product: float32 [2048, 4096], P(('layer', 'row'), 'col')
All inputs are finite; a program needn't handle non-finite values. No bound on the sum of `left_pattern` or of `right_pattern` or of `product_pattern` on one device may be relied on, other than what follows from the above.
Results may differ from a plain program's by a relative error of at most 0.000092.
Values sent between devices are 32-bit elements; how exact they have to be, the bound alone decides.
No kernel may reach another device: no remote copies, remote signals or barrier semaphores. Data moves between devices by JAX's collectives and lax.ppermute only.
A program may use at most 128 MiB of HBM per device.

v0:
```python
import jax
import jax.numpy as jnp
from jax import lax
from jax.sharding import PartitionSpec as P

BS = 64


def expand(pattern):
    return jnp.repeat(jnp.repeat(pattern.astype(jnp.float32), BS, axis=0), BS, axis=1)


def body(left_factor, right_factor, left_pattern, right_pattern, product_pattern):
    left = left_factor * expand(left_pattern)
    right = right_factor * expand(right_pattern)
    left_whole = lax.all_gather(left, "col", axis=1, tiled=True)
    partial_sum = jnp.dot(
        left_whole,
        lax.all_gather(right, "row", axis=0, tiled=True),
        preferred_element_type=jnp.float32,
        precision=lax.Precision.HIGHEST,
    )
    kept = partial_sum * expand(product_pattern)
    return lax.psum_scatter(kept, "layer", scatter_dimension=0, tiled=True)


def solution(mesh):
    return jax.shard_map(
        body,
        mesh=mesh,
        in_specs=(
            P("row", ("layer", "col")),
            P(("layer", "row"), "col"),
            P("row", ("layer", "col")),
            P(("layer", "row"), "col"),
            P("row", "col"),
        ),
        out_specs=P(("layer", "row"), "col"),
        check_vma=False,
    )
```

profile of v0, /device:TPU:8, one launch (start us, length us, event | category | flops | bytes accessed | tf_op | source)
XLA Modules:
  0.0 423.0 jit_solution(2757592346917892803)
XLA Ops:
  6.5 5.4 %copy.9 = f32[1024,1024]{0,1:T(8,128)} copy(f32[1024,1024]{1,0:T(8,128)} %param.6) | data formatting | bytes 8388608 | tf_op args[1]
  11.9 0.1 copy.8
  12.0 0.1 broadcast_in_dim.20
  12.1 0.1 reshape.20
  12.2 5.0 %bitcast_multiply_fusion = f32[1024,1024]{0,1:T(8,128)} fusion(f32[1024,1024]{0,1:T(8,128)} %copy.9, f32[1024,16]{0,1:T(8,128)S(1)} %reshape.20), kind=kLoop, calls=%fused_computation | loop fusion | flops 1048576 | bytes 8454144 | tf_op jit(solution)/shard_map/mul | solution.py:15
  17.2 0.0 all-gather.5.cloned.1.call-update
  17.2 0.0 all-gather.3.cloned.1.call-start
  17.3 1.9 copy.7
  19.2 0.0 copy-start.1
  19.3 0.1 broadcast_in_dim.18
  19.3 0.1 reshape.18
  19.4 1.5 bitcast_multiply_fusion.1
  21.0 0.0 all-gather.3.cloned.1.call-update
  21.0 0.0 reduce-scatter.2.cloned.1.call-start
  21.0 0.1 copy.10
  21.1 0.1 broadcast_in_dim.22
  21.2 0.1 reshape.22
  21.3 2.5 broadcast_in_dim.23
  23.8 5.4 %copy.11 = f32[1024,1024]{1,0:T(8,128)} copy(f32[1024,1024]{0,1:T(8,128)} %bitcast.13) | data formatting | bytes 8388608 | tf_op jit(solution)/shard_map/reshape | solution.py:10
  29.2 16.3 %all-gather.5.cloned.1.call-done = f32[2048,1024]{0,1:T(8,128)} async-done(((f32[1024,1024]{0,1:T(8,128)}), f32[2048,1024]{0,1:T(8,128)}) %all-gather.5.cloned.1.call-update) | async-done | bytes 8388624 | tf_op jit(solution)/shard_map/all_gather | solution.py:19
  45.5 88.7 %all-gather.3.cloned.1.call-done = f32[1024,2048]{0,1:T(8,128)} async-done(((f32[1024,512]{0,1:T(8,128)}), f32[1024,2048]{0,1:T(8,128)}) %all-gather.3.cloned.1.call-update) | async-done | bytes 8388624 | tf_op jit(solution)/shard_map/all_gather | solution.py:16
  134.2 57.5 %convolution_multiply_fusion = f32[1024,1024]{1,0:T(8,128)} fusion(f32[1024,1024]{1,0:T(8,128)} %copy.11, f32[1024,2048]{0,1:T(8,128)} %all-gather.3.cloned.1.call-done, f32[2048,1024]{0,1:T(8,128)} %all-gather.5.cloned.1.call-done), kind=kOutput, calls=%fused_computation.1 | convolution fusion | flops 25770852352 | bytes 25165824 | tf_op jit(solution)/shard_map/dot_general | solution.py:17
  191.7 0.0 reduce-scatter.2.cloned.1.call-update
  191.7 224.7 %reduce-scatter.2.cloned.1.call-done = f32[32,1024]{1,0:T(8,128)} async-done(((f32[1024,1024]{1,0:T(8,128)}), f32[32,1024]{1,0:T(8,128)}) %reduce-scatter.2.cloned.1.call-update) | async-done | bytes 131088 | tf_op jit(solution)/shard_map/reduce_scatter | solution.py:24
  (9 shorter events, 0.0 us)
Async XLA Ops:
  6.5 5.4 %copy-start = (s32[16,16]{1,0:T(8,128)S(1)}, s32[16,16]{1,0:T(8,128)}, u32[]{:S(2)}) copy-start(s32[16,16]{1,0:T(8,128)} %param.8) | copy-start | bytes 3076
  6.5 38.9 %all-gather.5.cloned.1.call-start = ((), (), s32[]{:S(2)}) async-start(), calls=%async_computation.2 | async-start | bytes 12582912 | tf_op jit(solution)/shard_map/all_gather | solution.py:19
  17.2 2.0 copy-start.2
  17.2 117.0 %all-gather.3.cloned.1.call-start = ((), (), s32[]{:S(2)}) async-start(), calls=%async_computation.1 | async-start | bytes 10485760 | tf_op jit(solution)/shard_map/all_gather | solution.py:16
  19.2 1.8 copy-start.1
  21.0 395.5 %reduce-scatter.2.cloned.1.call-start = ((), (), s32[]{:S(2)}) async-start(), calls=%async_computation.3 | async-start | bytes 4325376 | tf_op jit(solution)/shard_map/reduce_scatter | solution.py:24
Sparse Core Ops, SparseCore 0:
  17.4 28.0 all-gather.4
  47.3 86.8 all-gather.2
  191.8 224.5 reduce-scatter.1
where the time goes:
time: 423 us
  waiting for transfers between devices  330 us (78%)
  matrix products  57.5 us (14%)
  local copies, waits for them, and re-layouts  15.9 us (4%)
  between operations  13.2 us (3%)
  other arithmetic  6.55 us (2%)
    reduce_scatter x1, waiting for transfers between devices, body(): return lax.psum_scatter(kept, 'layer', scatter_dimension=0, tiled=True)  225 us
    all_gather x1, waiting for transfers between devices, body(): left_whole = lax.all_gather(left, 'col', axis=1, tiled=True)  88.7 us
    dot_general x1, matrix products, body(): jnp.dot(left_whole, lax.all_gather(right, 'row', axis=0, tiled=True), pre...  57.5 us
    all_gather x1, waiting for transfers between devices, body(): lax.all_gather(right, 'row', axis=0, tiled=True)  16.3 us
  transfers between devices with their start and end apart: 3, of which 3 were waited for; matrix products, arithmetic and copies ran while one was open for 3% of the time, Pallas kernels for 0%

commit v1 on v0

--- a/solution.py
+++ b/solution.py
@@ -16,7 +16,15 @@
     left_whole = lax.all_gather(left, "col", axis=1, tiled=True)
     partial_sum = jnp.dot(
         left_whole,
-        lax.all_gather(right, "row", axis=0, tiled=True),
+        jnp.concatenate(
+            lax.all_to_all(
+                jnp.stack([right] * lax.axis_size("row")),
+                axis_name="row",
+                split_axis=0,
+                concat_axis=0,
+            ),
+            axis=0,
+        ),
         preferred_element_type=jnp.float32,
         precision=lax.Precision.HIGHEST,
     )

time: 423 us -> 363 us (0.86)
  waiting for transfers between devices: 330 us -> 276 us
  matrix products: 57.5 us -> 31.9 us
  local copies, waits for them, and re-layouts: 15.9 us -> 24.6 us
  starting transfers between devices: 0.09 us -> 7.71 us
    all_gather x1, waiting for transfers between devices: 88.7 us -> 51.4 us  [body(): left_whole = lax.all_gather(left, 'col', axis=1, tiled=True)]
    dot_general x1, matrix products: 57.5 us -> 31.9 us  [body(): jnp.dot(left_whole, jnp.concatenate(lax.all_to_all(jnp.stack([right] * la...]
    all_gather x1 -> x0, waiting for transfers between devices: 16.3 us -> none  [body(): lax.all_gather(right, 'row', axis=0, tiled=True)]
    all_to_all x0 -> x1, local copies, waits for them, and re-layouts: none -> 8.75 us  [body(): lax.all_to_all(jnp.stack([right] * lax.axis_size('row')), axis_name='row'...]
    all_to_all x0 -> x1, starting transfers between devices: none -> 7.67 us  [body(): lax.all_to_all(jnp.stack([right] * lax.axis_size('row')), axis_name='row'...]
    another operation x0 -> x1, other arithmetic: none -> 4.29 us  [body(): jnp.stack([right] * lax.axis_size('row'))]
  transfers between devices with their start and end apart: 3 -> 3, of which waited for: 3 -> 2; matrix products, arithmetic and copies ran while one was open for 3% -> 8% of each run, Pallas kernels for 0% -> 0%
where the time goes in v1:
time: 363 us; the launch traced here: 362 us
  waiting for transfers between devices  276 us (76%)
  matrix products  31.9 us (9%)
  local copies, waits for them, and re-layouts  24.6 us (7%)
  between operations  13.5 us (4%)
  other arithmetic  8.5 us (2%)
  starting transfers between devices  7.71 us (2%)
    reduce_scatter x1, waiting for transfers between devices, body(): return lax.psum_scatter(kept, 'layer', scatter_dimension=0, tiled=True)  225 us
    all_gather x1, waiting for transfers between devices, body(): left_whole = lax.all_gather(left, 'col', axis=1, tiled=True)  51.4 us
    dot_general x1, matrix products, body(): jnp.dot(left_whole, jnp.concatenate(lax.all_to_all(jnp.stack([right] * la...  31.9 us
    all_to_all x1, local copies, waits for them, and re-layouts, body(): lax.all_to_all(jnp.stack([right] * lax.axis_size('row')), axis_name='row'...  8.75 us
    all_to_all x1, starting transfers between devices, body(): lax.all_to_all(jnp.stack([right] * lax.axis_size('row')), axis_name='row'...  7.67 us
    unnamed x8, local copies, waits for them, and re-layouts  7.32 us
  transfers between devices with their start and end apart: 3, of which 2 were waited for; matrix products, arithmetic and copies ran while one was open for 8% of the time, Pallas kernels for 0%

profile of v1, /device:TPU:8, one launch (start us, length us, event | category | flops | bytes accessed | tf_op | source)
XLA Modules:
  0.0 362.3 jit_solution(7018360422796637665)
XLA Ops:
  6.5 1.9 copy.12
  8.5 0.1 broadcast_in_dim.18
  8.6 0.1 reshape.21
  8.7 1.5 bitcast_multiply_fusion.1
  10.2 0.0 all-gather.2.cloned.1.call-update
  10.2 0.0 copy-start
  10.2 5.4 %copy.14 = f32[1024,1024]{0,1:T(8,128)} copy(f32[1024,1024]{1,0:T(8,128)} %param.6) | data formatting | bytes 8388608 | tf_op args[1]
  15.6 0.1 copy.13
  15.7 0.1 broadcast_in_dim.20
  15.8 0.1 reshape.23
  15.9 2.7 bitcast_multiply_fusion
  18.6 4.3 %pad_maximum_fusion = f32[2,1024,1024]{1,2,0:T(8,128)} fusion(f32[1,1024,1024]{1,2,0:T(8,128)S(1)} %bitcast.15), kind=kLoop, calls=%fused_computation | loop fusion | flops 2097152 | bytes 12582912 | tf_op jit(solution)/shard_map/stack | solution.py:21
  22.9 7.7 %all-to-all-start = ((f32[2,1024,1024]{1,2,0:T(8,128)}), f32[2,1024,1024]{1,2,0:T(8,128)}, u32[]{:S(2)}, u32[]{:S(2)}) async-start(f32[2,1024,1024]{1,2,0:T(8,128)} %pad_maximum_fusion), calls=%async_computation | async-start | bytes 16777216 | tf_op jit(solution)/shard_map/all_to_all | solution.py:20
  30.5 0.0 reduce-scatter.2.cloned.1.call-start
  30.6 0.1 copy.16
  30.7 0.1 broadcast_in_dim.22
  30.8 0.1 reshape.26
  30.9 2.5 broadcast_in_dim.23
  33.3 5.4 %copy.17 = f32[1024,1024]{1,0:T(8,128)} copy(f32[1024,1024]{0,1:T(8,128)} %bitcast.16) | data formatting | bytes 8388608 | tf_op jit(solution)/shard_map/reshape | solution.py:10
  38.7 8.7 %copy.15 = f32[2,1024,1024]{2,1,0:T(8,128)} copy(f32[2,1024,1024]{1,2,0:T(8,128)} %all-to-all-done) | data formatting | bytes 16777216 | tf_op jit(solution)/shard_map/all_to_all | solution.py:20
  47.5 51.4 %all-gather.2.cloned.1.call-done = f32[1024,2048]{0,1:T(8,128)} async-done(((f32[1024,512]{0,1:T(8,128)}), f32[1024,2048]{0,1:T(8,128)}) %all-gather.2.cloned.1.call-update) | async-done | bytes 8388624 | tf_op jit(solution)/shard_map/all_gather | solution.py:16
  98.9 31.9 %convolution_multiply_fusion = f32[1024,1024]{1,0:T(8,128)} fusion(f32[1024,1024]{1,0:T(8,128)} %copy.17, f32[1024,2048]{0,1:T(8,128)} %all-gather.2.cloned.1.call-done, f32[2048,1024]{1,0:T(8,128)} %bitcast.17), kind=kOutput, calls=%fused_computation.2 | convolution fusion | flops 25770852352 | bytes 25165824 | tf_op jit(solution)/shard_map/dot_general | solution.py:17
  130.8 0.0 reduce-scatter.2.cloned.1.call-update
  130.8 224.6 %reduce-scatter.2.cloned.1.call-done = f32[32,1024]{1,0:T(8,128)} async-done(((f32[1024,1024]{1,0:T(8,128)}), f32[32,1024]{1,0:T(8,128)}) %reduce-scatter.2.cloned.1.call-update) | async-done | bytes 131088 | tf_op jit(solution)/shard_map/reduce_scatter | solution.py:32
  (10 shorter events, 0.0 us)
Async XLA Ops:
  6.5 1.9 copy-start.2
  6.5 92.3 %all-gather.2.cloned.1.call-start = ((), (), s32[]{:S(2)}) async-start(), calls=%async_computation.2 | async-start | bytes 10485760 | tf_op jit(solution)/shard_map/all_gather | solution.py:16
  10.2 5.4 %copy-start = (s32[16,16]{1,0:T(8,128)S(1)}, s32[16,16]{1,0:T(8,128)}, u32[]{:S(2)}) copy-start(s32[16,16]{1,0:T(8,128)} %param.8) | copy-start | bytes 3076
  22.9 7.7 %copy-start.1 = (s32[16,16]{1,0:T(8,128)S(1)}, s32[16,16]{1,0:T(8,128)}, u32[]{:S(2)}) copy-start(s32[16,16]{1,0:T(8,128)} %param.9) | copy-start | bytes 3076
  22.9 15.9 %all-to-all-start = ((f32[2,1024,1024]{1,2,0:T(8,128)}), f32[2,1024,1024]{1,2,0:T(8,128)}, u32[]{:S(2)}, u32[]{:S(2)}) async-start(f32[2,1024,1024]{1,2,0:T(8,128)} %pad_maximum_fusion), calls=%async_computation | async-start | bytes 16777216 | tf_op jit(solution)/shard_map/all_to_all | solution.py:20
  30.5 324.9 %reduce-scatter.2.cloned.1.call-start = ((), (), s32[]{:S(2)}) async-start(), calls=%async_computation.3 | async-start | bytes 4325376 | tf_op jit(solution)/shard_map/reduce_scatter | solution.py:32
Sparse Core Ops, SparseCore 0:
  10.3 88.4 all-gather.1
  131.0 224.4 reduce-scatter.1
